TPU v7x, 32 devices: a whole 2x2x4 slice. The times are simulated.
32 devices in a mesh: row: 4 (over y, core), col: 8 (over z, x).
Axes of the slice: x: 2, y: 2, z: 4, core: 2. Of those that a mesh axis runs over, the one named last changes fastest.
Arguments:
- tokens: bfloat16 [1024, 16384], P('col', 'row'), may hold values from -6 to 6
- gate_weight: bfloat16 [16384, 26624], P('row', 'col'), may hold values from -0.046875 to 0.046875
- up_weight: bfloat16 [16384, 26624], P('row', 'col'), may hold values from -0.046875 to 0.046875
Outputs:
- hidden: bfloat16 [1024, 26624], P('row', 'col')
All inputs are finite; a program needn't handle non-finite values.
Results may differ from a plain program's by a relative error of at most 0.02.
Values may be sent and summed in bfloat16 or wider, within the bound.
No kernel may reach another device: no remote copies, remote signals or barrier semaphores. Data moves between devices by JAX's collectives and lax.ppermute only.
A program may use at most 192 MiB of HBM per device.

v0:
```python
import jax
import jax.numpy as jnp
from jax import lax
from jax.sharding import PartitionSpec as P


def on_device(tokens, gate_weight, up_weight):
    gathered = lax.all_gather(tokens, "col", axis=0, tiled=True)
    units = gate_weight.shape[1]
    gate_term = jnp.dot(gathered, gate_weight, preferred_element_type=jnp.float32)
    up_term = jnp.dot(gathered, up_weight, preferred_element_type=jnp.float32)
    summed = lax.psum_scatter(
        jnp.concatenate([gate_term, up_term], axis=1).astype(jnp.bfloat16),
        "row",
        scatter_dimension=0,
        tiled=True,
    ).astype(jnp.float32)
    gate = summed[:, :units]
    upper = summed[:, units:]
    return (jax.nn.silu(gate) * upper).astype(jnp.bfloat16)


def solution(mesh):
    placed = (P("col", "row"), P("row", "col"), P("row", "col"))
    return jax.shard_map(
        on_device, mesh=mesh, in_specs=placed, out_specs=P("row", "col"), check_vma=False
    )
```

profile of v0, /device:TPU:0, one launch (start us, length us, event | category | flops | bytes accessed | tf_op | source)
XLA Modules:
  0.0 333.6 jit_solution(17927107680310670530)
XLA Ops:
  6.5 0.0 all-gather.2.cloned.1.call-start
  6.5 0.7 all-gather.2.cloned.1.call-update
  7.3 0.0 reduce-scatter.2.cloned.1.call-start
  7.3 129.4 %all-gather.2.cloned.1.call-done = bf16[1024,4096]{1,0:T(8,128)(2,1)} async-done(((bf16[128,4096]{1,0:T(8,128)(2,1)}), bf16[1024,4096]{1,0:T(8,128)(2,1)}) %all-gather.2.cloned.1.call-update) | async-done | bytes 8388624 | tf_op jit(solution)/shard_map/all_gather | solution.py:8
  136.7 0.0 copy-start
  136.7 37.2 %convolution_convert_fusion = bf16[1024,3328]{1,0:T(8,128)(2,1)S(1)} fusion(bf16[1024,4096]{1,0:T(8,128)(2,1)} %all-gather.2.cloned.1.call-done, bf16[4096,3328]{1,0:T(8,128)(2,1)} %param.5), kind=kOutput, calls=%fused_computation.1 | convolution fusion | flops 27920695296 | bytes 42467328 | tf_op jit(solution)/shard_map/dot_general | solution.py:11
  173.9 0.0 copy-done
  173.9 33.8 %convolution_convert_fusion.1 = bf16[1024,3328]{1,0:T(8,128)(2,1)S(1)} fusion(bf16[1024,4096]{1,0:T(8,128)(2,1)S(1)} %copy-done, bf16[4096,3328]{1,0:T(8,128)(2,1)} %param.4), kind=kOutput, calls=%fused_computation.2 | convolution fusion | flops 27920695296 | bytes 42467328 | tf_op jit(solution)/shard_map/dot_general | solution.py:10
  207.7 9.0 %pad_maximum_fusion = bf16[1024,6656]{1,0:T(8,128)(2,1)} fusion(bf16[1024,3328]{1,0:T(8,128)(2,1)S(1)} %convolution_convert_fusion, bf16[1024,3328]{1,0:T(8,128)(2,1)S(1)} %convolution_convert_fusion.1), kind=kLoop, calls=%fused_computation | loop fusion | flops 27262976 | bytes 27262976 | tf_op jit(solution)/shard_map/concatenate | solution.py:13
  216.6 0.0 reduce-scatter.2.cloned.1.call-update
  216.6 105.1 %reduce-scatter.2.cloned.1.call-done = bf16[256,6656]{1,0:T(8,128)(2,1)} async-done(((bf16[1024,6656]{1,0:T(8,128)(2,1)}), bf16[256,6656]{1,0:T(8,128)(2,1)}) %reduce-scatter.2.cloned.1.call-update) | async-done | bytes 3407888 | tf_op jit(solution)/shard_map/reduce_scatter | solution.py:12
  321.8 2.7 convert_element_type.7
  324.5 2.2 fusion
Async XLA Ops:
  6.5 130.1 %all-gather.2.cloned.1.call-start = ((), (), s32[]{:S(2)}) async-start(), calls=%async_computation.1 | async-start | bytes 9437184 | tf_op jit(solution)/shard_map/all_gather | solution.py:8
  7.3 314.5 %reduce-scatter.2.cloned.1.call-start = ((), (), s32[]{:S(2)}) async-start(), calls=%async_computation.2 | async-start | bytes 17039360 | tf_op jit(solution)/shard_map/reduce_scatter | solution.py:12
  136.7 37.2 %copy-start = (bf16[1024,4096]{1,0:T(8,128)(2,1)S(1)}, bf16[1024,4096]{1,0:T(8,128)(2,1)}, u32[]{:S(2)}) copy-start(bf16[1024,4096]{1,0:T(8,128)(2,1)} %all-gather.2.cloned.1.call-done) | copy-start | bytes 25165828
Sparse Core Ops, SparseCore 0:
  9.5 127.1 all-gather.1
  216.8 104.9 reduce-scatter.1
where the time goes:
time: 334 us
  waiting for transfers between devices  235 us (70%)
  matrix products  70.9 us (21%)
  other arithmetic  13.9 us (4%)
  between operations  13.4 us (4%)
    all_gather x1, waiting for transfers between devices, on_device(): gathered = lax.all_gather(tokens, 'col', axis=0, tiled=True)  129 us
    reduce_scatter x1, waiting for transfers between devices, on_device(): lax.psum_scatter(jnp.concatenate([gate_term, up_term], axis=1).astype(jnp...  105 us
    dot_general x1, matrix products, on_device(): up_term = jnp.dot(gathered, up_weight, preferred_element_type=jnp.float32)  37.2 us
    dot_general x1, matrix products, on_device(): jnp.dot(gathered, gate_weight, preferred_element_type=jnp.float32)  33.8 us
    concatenate x1, other arithmetic, on_device(): jnp.concatenate([gate_term, up_term], axis=1).astype(jnp.bfloat16)  8.96 us
  transfers between devices with their start and end apart: 2, of which 2 were waited for; matrix products, arithmetic and copies ran while one was open for 0% of the time, Pallas kernels for 0%

commit v1 on v0

--- a/solution.py
+++ b/solution.py
@@ -4,8 +4,21 @@
 from jax.sharding import PartitionSpec as P
 
 
+def collect(array, axis, dim):
+    ways = lax.axis_size(axis)
+    up = [(d, (d + 1) % ways) for d in range(ways)]
+    down = [(d, (d - 1) % ways) for d in range(ways)]
+    earlier, later = ([array], [array])
+    for _ in range(ways // 2):
+        earlier.append(lax.ppermute(earlier[-1], axis, up))
+    for _ in range((ways - 1) // 2):
+        later.append(lax.ppermute(later[-1], axis, down))
+    line = jnp.concatenate([*earlier[::-1], *later[1:]], axis=dim)
+    return jnp.roll(line, (lax.axis_index(axis) - ways // 2) * array.shape[dim], axis=dim)
+
+
 def on_device(tokens, gate_weight, up_weight):
-    gathered = lax.all_gather(tokens, "col", axis=0, tiled=True)
+    gathered = collect(tokens, "col", 0)
     units = gate_weight.shape[1]
     gate_term = jnp.dot(gathered, gate_weight, preferred_element_type=jnp.float32)
     up_term = jnp.dot(gathered, up_weight, preferred_element_type=jnp.float32)

time: 334 us -> 400 us (1.20)
  starting transfers between devices: 0.04 us -> 60.9 us
  local copies, waits for them, and re-layouts: 0.01 us -> 27.2 us
  waiting for transfers between devices: 235 us -> 212 us
    all_gather x1 -> x0, waiting for transfers between devices: 129 us -> none  [on_device(): gathered = lax.all_gather(tokens, 'col', axis=0, tiled=True)]
    ppermute x0 -> x7, waiting for transfers between devices: none -> 105 us  [the longest x4 105 us: collect(): earlier.append(lax.ppermute(earlier[-1], axis, up))]
    ppermute x0 -> x7, starting transfers between devices: none -> 60.9 us  [the longest x3 52.9 us: collect(): later.append(lax.ppermute(later[-1], axis, down))]
    unnamed x2 -> x21, local copies, waits for them, and re-layouts: 0.01 us -> 26.2 us
  transfers between devices with their start and end apart: 2 -> 8, of which waited for: 2 -> 5; matrix products, arithmetic and copies ran while one was open for 0% -> 3% of each run, Pallas kernels for 0% -> 0%
where the time goes in v1:
time: 400 us; the launch traced here: 399 us
  waiting for transfers between devices  212 us (53%)
  matrix products  72.3 us (18%)
  starting transfers between devices  60.9 us (15%)
  local copies, waits for them, and re-layouts  27.2 us (7%)
  other arithmetic  14 us (4%)
  between operations  13.4 us (3%)
    reduce_scatter x1, waiting for transfers between devices, on_device(): lax.psum_scatter(jnp.concatenate([gate_term, up_term], axis=1).astype(jnp...  106 us
    ppermute x4, waiting for transfers between devices, collect(): earlier.append(lax.ppermute(earlier[-1], axis, up))  105 us
    ppermute x3, starting transfers between devices, collect(): later.append(lax.ppermute(later[-1], axis, down))  52.9 us
    dot_general x1, matrix products, on_device(): jnp.dot(gathered, gate_weight, preferred_element_type=jnp.float32)  36.2 us
    dot_general x1, matrix products, on_device(): up_term = jnp.dot(gathered, up_weight, preferred_element_type=jnp.float32)  36.1 us
    unnamed x21, local copies, waits for them, and re-layouts  26.2 us
    concatenate x1, other arithmetic, on_device(): jnp.concatenate([gate_term, up_term], axis=1).astype(jnp.bfloat16)  8.99 us
    ppermute x4, starting transfers between devices, collect(): earlier.append(lax.ppermute(earlier[-1], axis, up))  8.04 us
  transfers between devices with their start and end apart: 8, of which 5 were waited for; matrix products, arithmetic and copies ran while one was open for 3% of the time, Pallas kernels for 0%

profile of v1, /device:TPU:0, one launch (start us, length us, event | category | flops | bytes accessed | tf_op | source)
XLA Modules:
  0.0 399.4 jit_solution(13150401307096391865)
XLA Ops:
  6.5 0.0 copy-start
  6.5 0.0 reduce-scatter.2.cloned.1.call-start
  6.5 3.0 collective-permute-start
  9.5 26.5 %collective-permute-done = bf16[128,4096]{1,0:T(8,128)(2,1)S(1)} collective-permute-done((bf16[128,4096]{1,0:T(8,128)(2,1)}, bf16[128,4096]{1,0:T(8,128)(2,1)S(1)}, u32[]{:S(2)}, u32[]{:S(2)}) %collective-permute-start) | collective-permute-done | bytes 1048608 | tf_op jit(solution)/shard_map/ppermute | solution.py:13
  36.0 0.0 collective-permute-start.1
  36.0 4.7 %collective-permute-start.4 = (bf16[128,4096]{1,0:T(8,128)(2,1)}, bf16[128,4096]{1,0:T(8,128)(2,1)S(1)}, u32[]{:S(2)}, u32[]{:S(2)}) collective-permute-start(bf16[128,4096]{1,0:T(8,128)(2,1)} %param.3), channel_id=1, source_target_pairs={{0,7},{1,0},{2,1},{3,2},{4,3},{5,4},{6,5},{7,6},{8,15},{9,8},{10,9... | collective-permute-start | bytes 3145736 | tf_op jit(solution)/shard_map/ppermute | solution.py:15
  40.7 39.9 %collective-permute-done.1 = bf16[128,4096]{1,0:T(8,128)(2,1)S(1)} collective-permute-done((bf16[128,4096]{1,0:T(8,128)(2,1)S(1)}, bf16[128,4096]{1,0:T(8,128)(2,1)S(1)}, u32[]{:S(2)}, u32[]{:S(2)}) %collective-permute-start.1) | collective-permute-done | bytes 1048608 | tf_op jit(solution)/shard_map/ppermute | solution.py:13
  80.6 0.0 copy-start.1
  80.6 2.5 collective-permute-start.2
  83.1 0.0 collective-permute-done.4
  83.1 0.0 copy-done.1
  83.1 23.5 %collective-permute-start.5 = (bf16[128,4096]{1,0:T(8,128)(2,1)S(1)}, bf16[128,4096]{1,0:T(8,128)(2,1)}, u32[]{:S(2)}, u32[]{:S(2)}) collective-permute-start(bf16[128,4096]{1,0:T(8,128)(2,1)S(1)} %collective-permute-done.4), channel_id=1, source_target_pairs={{0,7},{1,0},{2,1},{3,2},{4,3},{5,4},{6,5},{7,6},{8,15},{9,8},{10,9... | collective-permute-start | bytes 3145736 | tf_op jit(solution)/shard_map/ppermute | solution.py:15
  106.6 20.2 %collective-permute-done.2 = bf16[128,4096]{1,0:T(8,128)(2,1)} collective-permute-done((bf16[128,4096]{1,0:T(8,128)(2,1)S(1)}, bf16[128,4096]{1,0:T(8,128)(2,1)}, u32[]{:S(2)}, u32[]{:S(2)}) %collective-permute-start.2) | collective-permute-done | bytes 1048608 | tf_op jit(solution)/shard_map/ppermute | solution.py:13
  126.8 2.6 collective-permute-start.3
  129.4 0.0 copy-start.2
  129.4 0.0 collective-permute-done.5
  129.4 24.6 %collective-permute-start.6 = (bf16[128,4096]{1,0:T(8,128)(2,1)}, bf16[128,4096]{1,0:T(8,128)(2,1)S(1)}, u32[]{:S(2)}, u32[]{:S(2)}) collective-permute-start(bf16[128,4096]{1,0:T(8,128)(2,1)} %collective-permute-done.5), channel_id=1, source_target_pairs={{0,7},{1,0},{2,1},{3,2},{4,3},{5,4},{6,5},{7,6},{8,15},{9,8},{10,9... | collective-permute-start | bytes 3145736 | tf_op jit(solution)/shard_map/ppermute | solution.py:15
  154.0 18.9 %collective-permute-done.3 = bf16[128,4096]{1,0:T(8,128)(2,1)} collective-permute-done((bf16[128,4096]{1,0:T(8,128)(2,1)}, bf16[128,4096]{1,0:T(8,128)(2,1)}, u32[]{:S(2)}, u32[]{:S(2)}) %collective-permute-start.3) | collective-permute-done | bytes 1048608 | tf_op jit(solution)/shard_map/ppermute | solution.py:13
  172.9 2.3 constant_dynamic-update-slice_fusion.15
  175.2 2.3 constant_dynamic-update-slice_fusion.14
  177.5 2.3 constant_dynamic-update-slice_fusion.13
  179.8 1.1 constant_dynamic-update-slice_fusion.12
  180.9 2.3 constant_dynamic-update-slice_fusion.11
  183.2 1.1 constant_dynamic-update-slice_fusion.10
  184.3 2.3 constant_dynamic-update-slice_fusion.9
  186.6 0.0 collective-permute-done.6
  186.6 1.1 constant_dynamic-update-slice_fusion.8
  187.7 2.4 constant_dynamic-update-slice_fusion.7
  190.1 2.3 constant_dynamic-update-slice_fusion.6
  192.4 0.0 copy-done.2
  192.4 1.1 constant_dynamic-update-slice_fusion.5
  193.4 1.1 constant_dynamic-update-slice_fusion.4
  194.5 0.0 copy-done
  194.5 1.1 constant_dynamic-update-slice_fusion.3
  195.7 1.1 constant_dynamic-update-slice_fusion.2
  196.8 2.3 constant_dynamic-update-slice_fusion.1
  199.1 1.0 constant_dynamic-update-slice_fusion
  200.1 36.1 %convolution_convert_fusion = bf16[1024,3328]{1,0:T(8,128)(2,1)S(1)} fusion(bf16[4096,3328]{1,0:T(8,128)(2,1)} %param.5, bf16[2048,4096]{1,0:T(8,128)(2,1)} %constant_dynamic-update-slice_fusion, s32[]{:T(128)S(6)} %select_n.14), kind=kOutput, calls=%fused_computation.1 | convolution fusion | flops 27920695296 | bytes 42467332 | tf_op jit(solution)/shard_map/dot_general | solution.py:24
  236.3 36.2 %convolution_convert_fusion.1 = bf16[1024,3328]{1,0:T(8,128)(2,1)S(1)} fusion(bf16[4096,3328]{1,0:T(8,128)(2,1)} %param.4, bf16[2048,4096]{1,0:T(8,128)(2,1)} %constant_dynamic-update-slice_fusion, s32[]{:T(128)S(6)} %select_n.14), kind=kOutput, calls=%fused_computation.2 | convolution fusion | flops 27920695296 | bytes 42467332 | tf_op jit(solution)/shard_map/dot_general | solution.py:23
  272.4 9.0 %pad_maximum_fusion = bf16[1024,6656]{1,0:T(8,128)(2,1)} fusion(bf16[1024,3328]{1,0:T(8,128)(2,1)S(1)} %convolution_convert_fusion, bf16[1024,3328]{1,0:T(8,128)(2,1)S(1)} %convolution_convert_fusion.1), kind=kLoop, calls=%fused_computation | loop fusion | flops 27262976 | bytes 27262976 | tf_op jit(solution)/shard_map/concatenate | solution.py:26
  281.4 0.0 reduce-scatter.2.cloned.1.call-update
  281.5 106.1 %reduce-scatter.2.cloned.1.call-done = bf16[256,6656]{1,0:T(8,128)(2,1)} async-done(((bf16[1024,6656]{1,0:T(8,128)(2,1)}), bf16[256,6656]{1,0:T(8,128)(2,1)}) %reduce-scatter.2.cloned.1.call-update) | async-done | bytes 3407888 | tf_op jit(solution)/shard_map/reduce_scatter | solution.py:25
  387.6 2.7 convert_element_type.7
  390.3 2.2 fusion.2
Async XLA Ops:
  6.5 188.0 %copy-start = (bf16[128,4096]{1,0:T(8,128)(2,1)S(1)}, bf16[128,4096]{1,0:T(8,128)(2,1)}, u32[]{:S(2)}) copy-start(bf16[128,4096]{1,0:T(8,128)(2,1)} %param.3) | copy-start | bytes 3145732
  6.5 381.0 %reduce-scatter.2.cloned.1.call-start = ((), (), s32[]{:S(2)}) async-start(), calls=%async_computation.1 | async-start | bytes 17039360 | tf_op jit(solution)/shard_map/reduce_scatter | solution.py:25
  6.5 29.4 %collective-permute-start = (bf16[128,4096]{1,0:T(8,128)(2,1)}, bf16[128,4096]{1,0:T(8,128)(2,1)S(1)}, u32[]{:S(2)}, u32[]{:S(2)}) collective-permute-start(bf16[128,4096]{1,0:T(8,128)(2,1)} %param.3), channel_id=1, source_target_pairs={{0,1},{1,2},{2,3},{3,4},{4,5},{5,6},{6,7},{7,0},{8,9},{9,10},{10,1... | collective-permute-start | bytes 3145736 | tf_op jit(solution)/shard_map/ppermute | solution.py:13
  36.0 44.6 %collective-permute-start.1 = (bf16[128,4096]{1,0:T(8,128)(2,1)S(1)}, bf16[128,4096]{1,0:T(8,128)(2,1)S(1)}, u32[]{:S(2)}, u32[]{:S(2)}) collective-permute-start(bf16[128,4096]{1,0:T(8,128)(2,1)S(1)} %collective-permute-done), channel_id=1, source_target_pairs={{0,1},{1,2},{2,3},{3,4},{4,5},{5,6},{6,7},{7,0},{8,9},{9,10},{10,1... | collective-permute-start | bytes 3145736 | tf_op jit(solution)/shard_map/ppermute | solution.py:13
  36.0 47.1 %collective-permute-start.4 = (bf16[128,4096]{1,0:T(8,128)(2,1)}, bf16[128,4096]{1,0:T(8,128)(2,1)S(1)}, u32[]{:S(2)}, u32[]{:S(2)}) collective-permute-start(bf16[128,4096]{1,0:T(8,128)(2,1)} %param.3), channel_id=1, source_target_pairs={{0,7},{1,0},{2,1},{3,2},{4,3},{5,4},{6,5},{7,6},{8,15},{9,8},{10,9... | collective-permute-start | bytes 3145736 | tf_op jit(solution)/shard_map/ppermute | solution.py:15
  80.6 2.5 copy-start.1
  80.6 46.2 %collective-permute-start.2 = (bf16[128,4096]{1,0:T(8,128)(2,1)S(1)}, bf16[128,4096]{1,0:T(8,128)(2,1)}, u32[]{:S(2)}, u32[]{:S(2)}) collective-permute-start(bf16[128,4096]{1,0:T(8,128)(2,1)S(1)} %collective-permute-done.1), channel_id=1, source_target_pairs={{0,1},{1,2},{2,3},{3,4},{4,5},{5,6},{6,7},{7,0},{8,9},{9,10},{10,1... | collective-permute-start | bytes 3145736 | tf_op jit(solution)/shard_map/ppermute | solution.py:13
  83.1 46.3 %collective-permute-start.5 = (bf16[128,4096]{1,0:T(8,128)(2,1)S(1)}, bf16[128,4096]{1,0:T(8,128)(2,1)}, u32[]{:S(2)}, u32[]{:S(2)}) collective-permute-start(bf16[128,4096]{1,0:T(8,128)(2,1)S(1)} %collective-permute-done.4), channel_id=1, source_target_pairs={{0,7},{1,0},{2,1},{3,2},{4,3},{5,4},{6,5},{7,6},{8,15},{9,8},{10,9... | collective-permute-start | bytes 3145736 | tf_op jit(solution)/shard_map/ppermute | solution.py:15
  126.8 46.1 %collective-permute-start.3 = (bf16[128,4096]{1,0:T(8,128)(2,1)}, bf16[128,4096]{1,0:T(8,128)(2,1)}, u32[]{:S(2)}, u32[]{:S(2)}) collective-permute-start(bf16[128,4096]{1,0:T(8,128)(2,1)} %collective-permute-done.2), channel_id=1, source_target_pairs={{0,1},{1,2},{2,3},{3,4},{4,5},{5,6},{6,7},{7,0},{8,9},{9,10},{10,1... | collective-permute-start | bytes 3145736 | tf_op jit(solution)/shard_map/ppermute | solution.py:13
  129.4 63.0 %copy-start.2 = (bf16[128,4096]{1,0:T(8,128)(2,1)S(1)}, bf16[128,4096]{1,0:T(8,128)(2,1)}, u32[]{:S(2)}) copy-start(bf16[128,4096]{1,0:T(8,128)(2,1)} %copy-done.1) | copy-start | bytes 3145732
  129.4 57.2 %collective-permute-start.6 = (bf16[128,4096]{1,0:T(8,128)(2,1)}, bf16[128,4096]{1,0:T(8,128)(2,1)S(1)}, u32[]{:S(2)}, u32[]{:S(2)}) collective-permute-start(bf16[128,4096]{1,0:T(8,128)(2,1)} %collective-permute-done.5), channel_id=1, source_target_pairs={{0,7},{1,0},{2,1},{3,2},{4,3},{5,4},{6,5},{7,6},{8,15},{9,8},{10,9... | collective-permute-start | bytes 3145736 | tf_op jit(solution)/shard_map/ppermute | solution.py:15
Sparse Core Ops, SparseCore 0:
  281.6 105.9 reduce-scatter.1
